TPU v7x, 1024 devices: a whole 4x4x32 slice. The times are simulated.
1024 devices in a mesh: dp: 64 (over z, core), tensor: 16 (over y, x).
Axes of the slice: x: 4, y: 4, z: 32, core: 2. Of those that a mesh axis runs over, the one named last changes fastest.
Arguments:
- inputs: bfloat16 [16384, 2560], P('dp'), may hold values from -16 to 16
- old_weight: bfloat16 [2560, 8192], P('dp', 'tensor'), may hold values from -0.125 to 0.125
- keep_cols: int32 [6144], replicated, may hold values from 0 to 8191, as said below
- owner: int32 [48], replicated, may hold values from 0 to 15, as said below
- out_grad: bfloat16 [16384, 6144], P('dp', 'tensor'), may hold values from -6 to 6
Outputs:
- projected: bfloat16 [16384, 6144], P('dp', 'tensor')
- gradient_input: bfloat16 [16384, 2560], P('dp', 'tensor')
- weight_grad: float32 [2560, 6144], P('dp', 'tensor')
Inputs may be any that keep to these rules, and one draw needn't show every extreme that they name: Each index t of tensor holds old columns [t * 4 * 128, (t + 1) * 4 * 128) and keeps exactly 384 of them, so blocks t * 3 to t * 3 + 2 of keep_cols come from holder t. Every owner receives exactly 3 blocks, and at most 2 blocks from one old holder; some owner receives 2 from one holder.
All inputs are finite; a program needn't handle non-finite values.
Results may differ from a plain program's by a relative error of at most 0.015.
Values may be sent and summed in bfloat16 or wider, within the bound.
No kernel may reach another device: no remote copies, remote signals or barrier semaphores. Data moves between devices by JAX's collectives and lax.ppermute only.
A program may use at most 32 MiB of HBM per device.

v0:
```python
import jax
import jax.numpy as jnp
from jax import lax
from jax.sharding import PartitionSpec as P


def local(inputs, old_weight, keep_cols, owner, out_grad):
    groups = lax.axis_size("tensor")
    myself = lax.axis_index("tensor")
    blocks = owner.shape[0]
    own_blocks = blocks // groups
    keep_table = keep_cols.reshape(blocks, 128)
    block_ids = jnp.arange(blocks, dtype=jnp.int32)
    earlier = block_ids[None, :] < block_ids[:, None]
    same_owner = owner[:, None] == owner[None, :]
    owner_rank = jnp.sum(same_owner & earlier, axis=1)
    ranks_here = jnp.arange(own_blocks, dtype=jnp.int32)
    mine_match = (owner[None, :] == myself) & (owner_rank[None, :] == ranks_here[:, None])
    mine_ids = jnp.sum(jnp.where(mine_match, block_ids[None, :], 0), axis=1)
    every_column = lax.all_gather(old_weight, "tensor", axis=1, tiled=True)
    new_stripe = jnp.take(every_column, keep_table[mine_ids].reshape(-1), axis=1)
    expanded_output = inputs.astype(jnp.float32)
    inverse_sigma = lax.rsqrt(
        jnp.mean(expanded_output * expanded_output, axis=1, keepdims=True) + 1e-05
    )
    centered_input = expanded_output * inverse_sigma
    normalized_rows = centered_input.astype(jnp.bfloat16)
    tokens, width = inputs.shape
    piece = lax.all_gather(new_stripe, "dp", axis=0, tiled=True)
    normed_cols = normalized_rows
    proj_sum = jnp.dot(normed_cols, piece, preferred_element_type=jnp.float32)
    partial_term = lax.dot_general(
        out_grad, piece, (((1,), (1,)), ((), ())), preferred_element_type=jnp.float32
    )
    back_sum = partial_term
    proj_sum, back_sum = (proj_sum, back_sum)
    projected = proj_sum.astype(jnp.bfloat16)
    share = width // groups
    reduced_total = lax.psum(back_sum.astype(jnp.bfloat16), "tensor").astype(jnp.float32)
    inner_product = jnp.mean(reduced_total * centered_input, axis=1, keepdims=True)
    complete_gradient = inverse_sigma * (reduced_total - centered_input * inner_product)
    gradient_input = lax.dynamic_slice_in_dim(complete_gradient, myself * share, share, 1).astype(
        jnp.bfloat16
    )
    normed_cols = normalized_rows
    weight_grad = lax.psum_scatter(
        lax.dot_general(
            normed_cols, out_grad, (((0,), (0,)), ((), ())), preferred_element_type=jnp.float32
        ),
        "dp",
        scatter_dimension=0,
        tiled=True,
    )
    return (projected, gradient_input, weight_grad)


def solution(mesh):
    placed = (P("dp", None), P("dp", "tensor"), P(), P(), P("dp", "tensor"))
    return jax.shard_map(
        local,
        mesh=mesh,
        in_specs=placed,
        out_specs=(P("dp", "tensor"), P("dp", "tensor"), P("dp", "tensor")),
        check_vma=False,
    )
```

profile of v0, /device:TPU:16, one launch (start us, length us, event | category | flops | bytes accessed | tf_op | source)
XLA Modules:
  0.0 566.7 jit_solution(10196239521160550581)
XLA Ops:
  7.2 0.0 copy-start
  7.2 0.0 all-gather.2.cloned.1.call-start
  7.2 0.9 convert_reduce_fusion
  8.1 0.7 broadcast_compare_fusion
  8.8 0.1 select_reduce_fusion
  8.9 1.3 gather_fusion
  10.3 0.9 copy.14
  11.2 34.2 %all_gather.6 = bf16[40,8192]{0,1:T(8,128)(2,1)S(1)} all-gather(bf16[40,512]{0,1:T(8,128)(2,1)S(1)} %copy.14), channel_id=1, replica_groups=mesh['dp'=64,'tensor'=16] {'tensor'}, dimensions={1}, use_global_device_ids=true | all-gather | bytes 696320 | tf_op jit(solution)/shard_map/all_gather | solution.py:20
  45.4 1.4 gather_fusion.1
  46.9 0.1 select_bitcast_fusion
  47.0 0.7 copy.15
  47.7 0.0 all-gather.2.cloned.1.call-update
  47.7 0.0 copy-start.3
  47.7 0.0 all-reduce.3.cloned.1.call-start
  47.8 135.3 %all-gather.2.cloned.1.call-done = bf16[2560,384]{1,0:T(8,128)(2,1)} async-done(((bf16[40,384]{1,0:T(8,128)(2,1)}), bf16[2560,384]{1,0:T(8,128)(2,1)}) %all-gather.2.cloned.1.call-update) | async-done | bytes 1966096 | tf_op jit(solution)/shard_map/all_gather | solution.py:29
  183.1 0.0 copy-done
  183.1 3.5 fusion
  186.6 0.0 all-reduce.3.cloned.1.call-update
  186.6 0.0 reduce-scatter.4.cloned.1.call-start
  186.7 0.0 copy-done.3
  186.7 0.6 copy.13
  187.3 0.4 fusion.1
  187.7 2.7 fusion.3
  190.4 0.0 reduce-scatter.4.cloned.1.call-update
  190.4 1.5 copy-done.2
  192.0 1.6 convolution_convert_fusion.1
  193.5 143.3 %all-reduce.3.cloned.1.call-done = bf16[256,2560]{0,1:T(8,128)(2,1)} async-done(((bf16[256,2560]{0,1:T(8,128)(2,1)}), bf16[256,2560]{0,1:T(8,128)(2,1)}) %all-reduce.3.cloned.1.call-update) | async-done | bytes 1310736 | tf_op jit(solution)/shard_map/psum | solution.py:39
  336.8 1.6 convert_element_type.30
  338.4 0.1 copy-done.1
  338.5 0.6 multiply_reduce_fusion
  339.1 0.7 fusion.7
  339.7 220.4 %reduce-scatter.4.cloned.1.call-done = f32[40,384]{1,0:T(8,128)} async-done(((f32[2560,384]{1,0:T(8,128)}), f32[40,384]{1,0:T(8,128)}) %reduce-scatter.4.cloned.1.call-update) | async-done | bytes 61456
  (9 shorter events, 0.1 us)
Async XLA Ops:
  7.2 175.9 %copy-start = (bf16[256,384]{1,0:T(8,128)(2,1)S(1)}, bf16[256,384]{1,0:T(8,128)(2,1)}, u32[]{:S(2)}) copy-start(bf16[256,384]{1,0:T(8,128)(2,1)} %param.9) | copy-start | bytes 589828
  7.2 175.9 %all-gather.2.cloned.1.call-start = ((), (), s32[]{:S(2)}) async-start(), calls=%async_computation.1 | async-start | bytes 1996800 | tf_op jit(solution)/shard_map/all_gather | solution.py:29
  47.7 139.0 %copy-start.3 = (bf16[256,2560]{1,0:T(8,128)(2,1)S(1)}, bf16[256,2560]{1,0:T(8,128)(2,1)}, u32[]{:S(2)}) copy-start(bf16[256,2560]{1,0:T(8,128)(2,1)} %param.5) | copy-start | bytes 3932164
  47.7 289.1 %all-reduce.3.cloned.1.call-start = ((), (), s32[]{:S(2)}) async-start(), calls=%async_computation.2 | async-start | bytes 2621440 | tf_op jit(solution)/shard_map/psum | solution.py:39
  186.6 373.5 %reduce-scatter.4.cloned.1.call-start = ((), (), s32[]{:S(2)}) async-start(), calls=%async_computation.3 | async-start | bytes 3993600
  190.4 1.5 copy-start.2
  336.8 1.7 copy-start.1
Sparse Core Ops, SparseCore 0:
  47.8 135.2 all-gather.1
  186.7 150.0 all-reduce.2
  340.8 219.3 reduce-scatter.3
where the time goes:
time: 567 us
  waiting for transfers between devices  499 us (88%)
  blocking collectives  34.2 us (6%)
  between operations  13.8 us (2%)
  matrix products  7.8 us (1%)
  local copies, waits for them, and re-layouts  6.57 us (1%)
    unnamed x4, waiting for transfers between devices  220 us
    psum x1, waiting for transfers between devices, local(): lax.psum(back_sum.astype(jnp.bfloat16), 'tensor').astype(jnp.float32)  143 us
    all_gather x1, waiting for transfers between devices, local(): piece = lax.all_gather(new_stripe, 'dp', axis=0, tiled=True)  135 us
    all_gather x1, blocking collectives, local(): every_column = lax.all_gather(old_weight, 'tensor', axis=1, tiled=True)  34.2 us
  transfers between devices with their start and end apart: 3, of which 3 were waited for; matrix products, arithmetic and copies ran while one was open for 1% of the time, Pallas kernels for 0%

commit v1 on v0

v1 whole, which is shorter than its diff:
```python
import jax
import jax.numpy as jnp
from jax import lax
from jax.sharding import Mesh
from jax.sharding import PartitionSpec as P

ZL = 4
DP = ("zh", "zl", "c")
TN = ("y", "x")


def _split_hi_lo(s):
    hi = lax.reduce_precision(s, exponent_bits=8, mantissa_bits=7)
    lo = s - hi
    return hi.astype(jnp.bfloat16), lo.astype(jnp.bfloat16)


def local(inputs, old_weight, keep_cols, owner, out_grad):
    n_t = lax.axis_size(TN)
    n_zh, n_zl, n_c = lax.axis_size("zh"), lax.axis_size("zl"), lax.axis_size("c")
    n_z = n_zh * n_zl
    me = lax.axis_index(TN)
    blocks = owner.shape[0]
    own_blocks = blocks // n_t
    old_cols = old_weight.shape[1]
    rows = old_weight.shape[0]
    tokens, width = inputs.shape
    share = width // n_t

    keep_table = keep_cols.reshape(blocks, 128)
    block_ids = jnp.arange(blocks, dtype=jnp.int32)
    holder_of = block_ids // own_blocks
    earlier = block_ids[None, :] < block_ids[:, None]
    same_pair = (owner[:, None] == owner[None, :]) & (holder_of[:, None] == holder_of[None, :])
    slot_of = jnp.sum(same_pair & earlier, axis=1)
    same_owner = owner[:, None] == owner[None, :]
    owner_rank = jnp.sum(same_owner & earlier, axis=1)

    mine = me * own_blocks + jnp.arange(own_blocks, dtype=jnp.int32)
    dest = jnp.arange(n_t, dtype=jnp.int32)
    slots = jnp.arange(2, dtype=jnp.int32)
    match = (owner[mine][None, None, :] == dest[:, None, None]) & (
        slot_of[mine][None, None, :] == slots[None, :, None]
    )
    pick = jnp.sum(jnp.where(match, mine[None, None, :], 0), axis=2)
    pick = jnp.where(jnp.any(match, axis=2), pick, mine[0])
    local_cols = keep_table[pick] - me * old_cols
    local_cols = jnp.clip(local_cols, 0, old_cols - 1)
    send = jnp.take(old_weight, local_cols.reshape(-1), axis=1).reshape(rows, n_t, 2 * 128)
    send = jnp.transpose(send, (1, 0, 2))
    recv = lax.all_to_all(send, TN, 0, 0, tiled=False)

    k_ids = jnp.arange(own_blocks, dtype=jnp.int32)
    mine_match = (owner[None, :] == me) & (owner_rank[None, :] == k_ids[:, None])
    my_blocks = jnp.sum(jnp.where(mine_match, block_ids[None, :], 0), axis=1)
    h_k = holder_of[my_blocks]
    s_k = slot_of[my_blocks]
    recv4 = recv.reshape(n_t, rows, 2, 128)
    new_stripe = jnp.concatenate(
        [recv4[h_k[k], :, s_k[k], :] for k in range(own_blocks)], axis=1
    )

    piece = lax.all_gather(new_stripe, ("zh", "zl"), axis=0, tiled=True)
    piece = lax.all_gather(piece, "c", axis=0, tiled=True)
    piece = piece.reshape(n_c, n_z, rows, -1).transpose(1, 0, 2, 3).reshape(width, -1)

    x = inputs.astype(jnp.float32)
    inv = lax.rsqrt(jnp.mean(x * x, axis=1, keepdims=True) + 1e-05)
    xhat = x * inv
    normed = xhat.astype(jnp.bfloat16)

    wg = lax.dot_general(normed, out_grad, (((0,), (0,)), ((), ())), preferred_element_type=jnp.float32)
    wg = wg.reshape(n_zh, n_zl, n_c, rows, -1)
    wg = lax.all_to_all(wg, "c", 2, 2, tiled=False).sum(2)
    wg = lax.all_to_all(wg.astype(jnp.bfloat16), "zl", 1, 1, tiled=False).astype(jnp.float32).sum(1)
    wg = lax.all_to_all(wg.astype(jnp.bfloat16), "zh", 0, 0, tiled=False).astype(jnp.float32).sum(0)

    projected = jnp.dot(normed, piece, preferred_element_type=jnp.float32).astype(jnp.bfloat16)

    partial = lax.dot_general(
        out_grad, piece, (((1,), (1,)), ((), ())), preferred_element_type=jnp.float32
    ).astype(jnp.bfloat16)
    s_part = jnp.sum(partial.astype(jnp.float32) * xhat, axis=1)
    hi, lo = _split_hi_lo(s_part)
    extra_len = 4 * share
    extra = jnp.concatenate([hi, lo, jnp.zeros((extra_len - 2 * tokens,), jnp.bfloat16)])
    extra = jnp.broadcast_to(extra.reshape(1, 4, share), (n_t, 4, share))
    payload = jnp.transpose(partial.reshape(tokens, n_t, share), (1, 0, 2))
    payload = jnp.concatenate([payload, extra], axis=1)
    got = lax.all_to_all(payload, TN, 0, 0, tiled=False)
    dn = jnp.sum(got[:, :tokens].astype(jnp.float32), axis=0)
    ex = got[:, tokens:].reshape(n_t, extra_len)
    s_tot = jnp.sum(
        ex[:, :tokens].astype(jnp.float32) + ex[:, tokens:2 * tokens].astype(jnp.float32), axis=0
    )
    inner = (s_tot / width)[:, None]
    xhat_me = lax.dynamic_slice_in_dim(xhat, me * share, share, 1)
    gradient_input = (inv * (dn - xhat_me * inner)).astype(jnp.bfloat16)
    return (projected, gradient_input, wg)


def solution(mesh):
    n_dp, n_t = mesh.devices.shape
    devs = mesh.devices.reshape(n_dp // (2 * ZL), ZL, 2, 4, n_t // 4)
    m = Mesh(devs, ("zh", "zl", "c", "y", "x"))
    placed = (P(DP, None), P(DP, TN), P(), P(), P(DP, TN))
    return jax.shard_map(
        local,
        mesh=m,
        in_specs=placed,
        out_specs=(P(DP, TN), P(DP, TN), P(DP, TN)),
        check_vma=False,
    )
```

time: 567 us -> 285 us (0.50)
  the two profiles are of different devices: /device:TPU:16 before, /device:TPU:32 now
where the time goes in v1:
time: 285 us; the launch traced here: 284 us
  waiting for transfers between devices  89.7 us (31%)
  blocking collectives  70.7 us (25%)
  starting transfers between devices  54.8 us (19%)
  between operations  25.8 us (9%)
  local copies, waits for them, and re-layouts  25 us (9%)
  other arithmetic  11.4 us (4%)
  matrix products  6.27 us (2%)
    all_gather x1, blocking collectives, local(): piece = lax.all_gather(new_stripe, ('zh', 'zl'), axis=0, tiled=True)  70.7 us
    all_to_all x1, waiting for transfers between devices, local(): lax.all_to_all(wg.astype(jnp.bfloat16), 'zh', 0, 0, tiled=False)  32.6 us
    all_to_all x1, waiting for transfers between devices, local(): got = lax.all_to_all(payload, TN, 0, 0, tiled=False)  29.4 us
    all_to_all x1, starting transfers between devices, local(): lax.all_to_all(wg.astype(jnp.bfloat16), 'zh', 0, 0, tiled=False)  21.6 us
    all_gather x1, waiting for transfers between devices, local(): piece = lax.all_gather(piece, 'c', axis=0, tiled=True)  21.3 us
    all_to_all x1, starting transfers between devices, local(): lax.all_to_all(wg.astype(jnp.bfloat16), 'zl', 1, 1, tiled=False)  13.6 us
    gather x2, local copies, waits for them, and re-layouts, local(): jnp.take(old_weight, local_cols.reshape(-1), axis=1)  12.5 us
    all_to_all x1, starting transfers between devices, local(): recv = lax.all_to_all(send, TN, 0, 0, tiled=False)  7.04 us
  transfers between devices with their start and end apart: 6, of which 4 were waited for; matrix products, arithmetic and copies ran while one was open for 13% of the time, Pallas kernels for 0%

profile of v1, /device:TPU:32, one launch (start us, length us, event | category | flops | bytes accessed | tf_op | source)
XLA Modules:
  0.0 283.7 jit_solution(7082011449633301964)
XLA Ops:
  7.2 1.6 copy.46
  9.2 0.9 fusion.2
  10.1 2.3 copy.59
  12.3 5.6 %all-to-all-start.2 = ((f32[8,4,2,40,384]{4,3,1,0,2:T(8,128)}), f32[8,4,2,40,384]{4,3,1,0,2:T(8,128)}, u32[]{:S(2)}, u32[]{:S(2)}) async-start(f32[8,4,2,40,384]{4,3,1,0,2:T(8,128)} %copy.59), calls=%async_computation.2 | async-start | bytes 7864320 | tf_op jit(solution)/shard_map/all_to_all | solution.py:74
  18.4 0.6 gather_fusion
  19.0 0.6 gather_fusion.1
  20.2 0.6 gather_fusion.2
  21.0 12.1 %gather_fusion.3 = bf16[4096,40]{1,0:T(8,128)(2,1)S(1)} fusion(bf16[40,512]{0,1:T(8,128)(2,1)S(1)} %copy.49, s32[4096]{0:T(1024)S(1)} %broadcast_clamp_fusion), kind=kCustom, calls=%fused_computation.3 | custom fusion | bytes 671744 | tf_op jit(solution)/shard_map/jit(_take)/gather | solution.py:49
  33.5 0.8 select_bitcast_fusion
  34.2 7.0 %all-to-all-start = ((bf16[16,40,256]{2,1,0:T(8,128)(2,1)}), bf16[16,40,256]{2,1,0:T(8,128)(2,1)S(1)}, u32[]{:S(2)}, u32[]{:S(2)}) async-start(bf16[16,40,256]{2,1,0:T(8,128)(2,1)} %select_bitcast_fusion), calls=%async_computation | async-start | bytes 655360 | tf_op jit(solution)/shard_map/all_to_all | solution.py:51
  41.3 2.5 reduce_sum.113
  43.8 1.1 copy.60
  44.9 6.4 %all-to-all-done = bf16[16,40,256]{2,1,0:T(8,128)(2,1)S(1)} async-done(((bf16[16,40,256]{2,1,0:T(8,128)(2,1)}), bf16[16,40,256]{2,1,0:T(8,128)(2,1)S(1)}, u32[]{:S(2)}, u32[]{:S(2)}) %all-to-all-start) | async-done | bytes 327712 | tf_op jit(solution)/shard_map/all_to_all | solution.py:51
  51.3 13.6 %all-to-all-start.3 = ((bf16[8,4,40,384]{3,2,0,1:T(8,128)(2,1)}), bf16[8,4,40,384]{3,2,0,1:T(8,128)(2,1)}, u32[]{:S(2)}, u32[]{:S(2)}) async-start(bf16[8,4,40,384]{3,2,0,1:T(8,128)(2,1)} %copy.60), calls=%async_computation.3 | async-start | bytes 1966080 | tf_op jit(solution)/shard_map/all_to_all | solution.py:75
  65.0 0.6 gather_fusion.5
  65.6 0.6 gather_fusion.4
  66.2 0.6 fusion.12
  70.7 0.6 fusion.11
  79.2 70.7 %all_gather.6 = bf16[1280,384]{1,0:T(8,128)(2,1)} all-gather(bf16[40,384]{1,0:T(8,128)(2,1)S(1)} %pad_maximum_fusion.1), channel_id=1, replica_groups=mesh['zh'=8,'zl'=4,'c'=2,'y'=4,'x'=4] {'zh','zl'}, dimensions={0}, use_global_device_ids=true | all-gather | bytes 1013760 | tf_op jit(solution)/shard_map/all_gather | solution.py:63
  149.9 21.3 %all-gather.2.cloned.1.call-done = bf16[2560,384]{1,0:T(8,128)(2,1)} async-done(((bf16[1280,384]{1,0:T(8,128)(2,1)}), bf16[2560,384]{1,0:T(8,128)(2,1)}) %all-gather.2.cloned.1.call-update) | async-done | bytes 1966096 | tf_op jit(solution)/shard_map/all_gather | solution.py:64
  171.1 1.7 copy.54
  172.9 2.3 convert_multiply_fusion
  175.5 1.6 pad_maximum_fusion
  177.1 6.8 %all-to-all-start.1 = ((bf16[16,260,160]{1,2,0:T(8,128)(2,1)}), bf16[16,260,160]{1,2,0:T(8,128)(2,1)S(1)}, u32[]{:S(2)}, u32[]{:S(2)}) async-start(bf16[16,260,160]{1,2,0:T(8,128)(2,1)} %pad_maximum_fusion), calls=%async_computation.1 | async-start | bytes 3932160 | tf_op jit(solution)/shard_map/all_to_all | solution.py:90
  183.9 2.1 reduce_sum.114
  186.0 29.4 %all-to-all-done.1 = bf16[16,260,160]{1,2,0:T(8,128)(2,1)S(1)} async-done(((bf16[16,260,160]{1,2,0:T(8,128)(2,1)}), bf16[16,260,160]{1,2,0:T(8,128)(2,1)S(1)}, u32[]{:S(2)}, u32[]{:S(2)}) %all-to-all-start.1) | async-done | bytes 1331232 | tf_op jit(solution)/shard_map/all_to_all | solution.py:90
  215.4 21.6 %all-to-all-start.4 = ((bf16[8,40,384]{2,1,0:T(8,128)(2,1)}), bf16[8,40,384]{2,1,0:T(8,128)(2,1)}, u32[]{:S(2)}, u32[]{:S(2)}) async-start(bf16[8,40,384]{2,1,0:T(8,128)(2,1)} %reduce_sum.114), calls=%async_computation.4 | async-start | bytes 491520 | tf_op jit(solution)/shard_map/all_to_all | solution.py:76
  237.1 3.1 %convolution_convert_fusion.1 = bf16[256,384]{1,0:T(8,128)(2,1)} fusion(bf16[2560,384]{1,0:T(8,128)(2,1)} %bitcast.52, f32[256]{0:T(256)S(1)} %add_rsqrt_fusion, bf16[256,2560]{0,1:T(8,128)(2,1)S(1)} %copy.46), kind=kOutput, calls=%fused_computation.13 | convolution fusion | flops 505380864 | bytes 3474432 | tf_op jit(solution)/shard_map/dot_general | solution.py:78
  240.3 0.4 copy.57
  241.0 1.6 multiply_convert_fusion
  242.6 32.6 %all-to-all-done.4 = bf16[8,40,384]{2,1,0:T(8,128)(2,1)} async-done(((bf16[8,40,384]{2,1,0:T(8,128)(2,1)}), bf16[8,40,384]{2,1,0:T(8,128)(2,1)}, u32[]{:S(2)}, u32[]{:S(2)}) %all-to-all-start.4) | async-done | bytes 245792 | tf_op jit(solution)/shard_map/all_to_all | solution.py:76
  275.2 1.6 convert_reduce_fusion.1
  (56 shorter events, 2.8 us)
Async XLA Ops:
  7.2 2.0 copy-start
  12.3 5.7 %copy-start.1 = (s32[48]{0:T(128)S(1)}, s32[48]{0:T(128)}, u32[]{:S(2)}) copy-start(s32[48]{0:T(128)} %param.8) | copy-start | bytes 580
  12.3 7.9 %copy-start.3 = (s32[6144]{0:T(1024)S(1)}, s32[6144]{0:T(1024)}, u32[]{:S(2)}) copy-start(s32[6144]{0:T(1024)} %param.7) | copy-start | bytes 73732
  12.3 8.5 %copy-start.4 = (bf16[40,512]{1,0:T(8,128)(2,1)S(1)}, bf16[40,512]{1,0:T(8,128)(2,1)}, u32[]{:S(2)}) copy-start(bf16[40,512]{1,0:T(8,128)(2,1)} %param.6) | copy-start | bytes 122884
  12.3 21.9 %all-to-all-start.2 = ((f32[8,4,2,40,384]{4,3,1,0,2:T(8,128)}), f32[8,4,2,40,384]{4,3,1,0,2:T(8,128)}, u32[]{:S(2)}, u32[]{:S(2)}) async-start(f32[8,4,2,40,384]{4,3,1,0,2:T(8,128)} %copy.59), calls=%async_computation.2 | async-start | bytes 7864320 | tf_op jit(solution)/shard_map/all_to_all | solution.py:74
  34.2 17.1 %all-to-all-start = ((bf16[16,40,256]{2,1,0:T(8,128)(2,1)}), bf16[16,40,256]{2,1,0:T(8,128)(2,1)S(1)}, u32[]{:S(2)}, u32[]{:S(2)}) async-start(bf16[16,40,256]{2,1,0:T(8,128)(2,1)} %select_bitcast_fusion), calls=%async_computation | async-start | bytes 655360 | tf_op jit(solution)/shard_map/all_to_all | solution.py:51
  51.3 125.8 %all-to-all-start.3 = ((bf16[8,4,40,384]{3,2,0,1:T(8,128)(2,1)}), bf16[8,4,40,384]{3,2,0,1:T(8,128)(2,1)}, u32[]{:S(2)}, u32[]{:S(2)}) async-start(bf16[8,4,40,384]{3,2,0,1:T(8,128)(2,1)} %copy.60), calls=%async_computation.3 | async-start | bytes 1966080 | tf_op jit(solution)/shard_map/all_to_all | solution.py:75
  65.0 106.1 %all-gather.2.cloned.1.call-start = ((), (), s32[]{:S(2)}) async-start(), calls=%async_computation.5 | async-start | bytes 2949120 | tf_op jit(solution)/shard_map/all_gather | solution.py:64
  172.8 2.3 copy-start.2
  177.1 38.3 %all-to-all-start.1 = ((bf16[16,260,160]{1,2,0:T(8,128)(2,1)}), bf16[16,260,160]{1,2,0:T(8,128)(2,1)S(1)}, u32[]{:S(2)}, u32[]{:S(2)}) async-start(bf16[16,260,160]{1,2,0:T(8,128)(2,1)} %pad_maximum_fusion), calls=%async_computation.1 | async-start | bytes 3932160 | tf_op jit(solution)/shard_map/all_to_all | solution.py:90
  215.4 59.8 %all-to-all-start.4 = ((bf16[8,40,384]{2,1,0:T(8,128)(2,1)}), bf16[8,40,384]{2,1,0:T(8,128)(2,1)}, u32[]{:S(2)}, u32[]{:S(2)}) async-start(bf16[8,40,384]{2,1,0:T(8,128)(2,1)} %reduce_sum.114), calls=%async_computation.4 | async-start | bytes 491520 | tf_op jit(solution)/shard_map/all_to_all | solution.py:76
Sparse Core Ops, SparseCore 0:
  150.0 21.0 all-gather.1

commit v2 on v1

--- a/solution.py
+++ b/solution.py
@@ -3,6 +3,7 @@
 from jax import lax
 from jax.sharding import Mesh
 from jax.sharding import PartitionSpec as P
+
 
 ZL = 4
 DP = ("zh", "zl", "c")
@@ -15,7 +16,7 @@
     return hi.astype(jnp.bfloat16), lo.astype(jnp.bfloat16)
 
 
-def local(inputs, old_weight, keep_cols, owner, out_grad):
+def _body(inputs, old_weight, keep_cols, owner, out_grad):
     n_t = lax.axis_size(TN)
     n_zh, n_zl, n_c = lax.axis_size("zh"), lax.axis_size("zl"), lax.axis_size("c")
     n_z = n_zh * n_zl
@@ -46,8 +47,12 @@
     pick = jnp.where(jnp.any(match, axis=2), pick, mine[0])
     local_cols = keep_table[pick] - me * old_cols
     local_cols = jnp.clip(local_cols, 0, old_cols - 1)
-    send = jnp.take(old_weight, local_cols.reshape(-1), axis=1).reshape(rows, n_t, 2 * 128)
-    send = jnp.transpose(send, (1, 0, 2))
+    onehot = (
+        jnp.arange(old_cols, dtype=jnp.int32)[:, None, None] == local_cols.reshape(1, n_t, 256)
+    ).astype(old_weight.dtype)
+    send = jnp.einsum(
+        "rc,ctj->trj", old_weight, onehot, preferred_element_type=jnp.float32
+    ).astype(old_weight.dtype)
     recv = lax.all_to_all(send, TN, 0, 0, tiled=False)
 
     k_ids = jnp.arange(own_blocks, dtype=jnp.int32)
@@ -73,7 +78,8 @@
     wg = wg.reshape(n_zh, n_zl, n_c, rows, -1)
     wg = lax.all_to_all(wg, "c", 2, 2, tiled=False).sum(2)
     wg = lax.all_to_all(wg.astype(jnp.bfloat16), "zl", 1, 1, tiled=False).astype(jnp.float32).sum(1)
-    wg = lax.all_to_all(wg.astype(jnp.bfloat16), "zh", 0, 0, tiled=False).astype(jnp.float32).sum(0)
+    wg = lax.all_to_all(wg.astype(jnp.bfloat16), "zh", 0, 0, tiled=False)
+    wg = wg.astype(jnp.float32).sum(0)
 
     projected = jnp.dot(normed, piece, preferred_element_type=jnp.float32).astype(jnp.bfloat16)
 
@@ -105,7 +111,7 @@
     m = Mesh(devs, ("zh", "zl", "c", "y", "x"))
     placed = (P(DP, None), P(DP, TN), P(), P(), P(DP, TN))
     return jax.shard_map(
-        local,
+        _body,
         mesh=m,
         in_specs=placed,
         out_specs=(P(DP, TN), P(DP, TN), P(DP, TN)),

time: 285 us -> 273 us (0.958)
  local copies, waits for them, and re-layouts: 25 us -> 12.4 us
    gather x7 -> x5, local copies, waits for them, and re-layouts: 15.6 us -> 3.13 us  [the longest x1 0.64 us: _body(): s_k = slot_of[my_blocks]]
    dot_general x3 -> x4, matrix products: 6.27 us -> 8.51 us  [the longest x1 3.11 us: _body(): jnp.dot(normed, piece, preferred_element_type=jnp.float32)]
  transfers between devices with their start and end apart: 6 -> 6, of which waited for: 4 -> 4; matrix products, arithmetic and copies ran while one was open for 13% -> 9% of each run, Pallas kernels for 0% -> 0%
where the time goes in v2:
time: 273 us; the launch traced here: 272 us
  waiting for transfers between devices  89.7 us (33%)
  blocking collectives  70.7 us (26%)
  starting transfers between devices  54.8 us (20%)
  between operations  25.7 us (9%)
  local copies, waits for them, and re-layouts  12.4 us (5%)
  other arithmetic  10.7 us (4%)
  matrix products  8.51 us (3%)
    all_gather x1, blocking collectives, _body(): piece = lax.all_gather(new_stripe, ('zh', 'zl'), axis=0, tiled=True)  70.7 us
    all_to_all x1, waiting for transfers between devices, _body(): wg = lax.all_to_all(wg.astype(jnp.bfloat16), 'zh', 0, 0, tiled=False)  32.6 us
    all_to_all x1, waiting for transfers between devices, _body(): got = lax.all_to_all(payload, TN, 0, 0, tiled=False)  29.4 us
    all_to_all x1, starting transfers between devices, _body(): wg = lax.all_to_all(wg.astype(jnp.bfloat16), 'zh', 0, 0, tiled=False)  21.6 us
    all_gather x1, waiting for transfers between devices, _body(): piece = lax.all_gather(piece, 'c', axis=0, tiled=True)  21.3 us
    all_to_all x1, starting transfers between devices, _body(): lax.all_to_all(wg.astype(jnp.bfloat16), 'zl', 1, 1, tiled=False)  13.7 us
    all_to_all x1, starting transfers between devices, _body(): recv = lax.all_to_all(send, TN, 0, 0, tiled=False)  7.03 us
    all_to_all x1, starting transfers between devices, _body(): got = lax.all_to_all(payload, TN, 0, 0, tiled=False)  6.81 us
  transfers between devices with their start and end apart: 6, of which 4 were waited for; matrix products, arithmetic and copies ran while one was open for 9% of the time, Pallas kernels for 0%

profile of v2, /device:TPU:32, one launch (start us, length us, event | category | flops | bytes accessed | tf_op | source)
XLA Modules:
  0.0 272.5 jit_solution(8054885456460143957)
XLA Ops:
  7.2 1.6 copy.40
  8.8 0.4 fusion.2
  9.2 0.9 fusion.6
  10.1 2.3 copy.51
  12.3 5.6 %all-to-all-start.2 = ((f32[8,4,2,40,384]{4,3,1,0,2:T(8,128)}), f32[8,4,2,40,384]{4,3,1,0,2:T(8,128)}, u32[]{:S(2)}, u32[]{:S(2)}) async-start(f32[8,4,2,40,384]{4,3,1,0,2:T(8,128)} %copy.51), calls=%async_computation.2 | async-start | bytes 7864320 | tf_op jit(solution)/shard_map/all_to_all | solution.py:79
  18.4 0.6 gather_fusion
  19.0 0.6 gather_fusion.1
  20.2 0.6 gather_fusion.2
  20.8 2.3 fusion.4
  23.1 7.0 %all-to-all-start = ((bf16[16,40,256]{2,1,0:T(8,128)(2,1)}), bf16[16,40,256]{2,1,0:T(8,128)(2,1)S(1)}, u32[]{:S(2)}, u32[]{:S(2)}) async-start(bf16[16,40,256]{2,1,0:T(8,128)(2,1)} %fusion.4), calls=%async_computation | async-start | bytes 655360 | tf_op jit(solution)/shard_map/all_to_all | solution.py:56
  30.1 2.5 reduce_sum.113
  32.6 1.1 copy.52
  33.7 6.4 %all-to-all-done = bf16[16,40,256]{2,1,0:T(8,128)(2,1)S(1)} async-done(((bf16[16,40,256]{2,1,0:T(8,128)(2,1)}), bf16[16,40,256]{2,1,0:T(8,128)(2,1)S(1)}, u32[]{:S(2)}, u32[]{:S(2)}) %all-to-all-start) | async-done | bytes 327712 | tf_op jit(solution)/shard_map/all_to_all | solution.py:56
  40.2 13.7 %all-to-all-start.3 = ((bf16[8,4,40,384]{3,2,0,1:T(8,128)(2,1)}), bf16[8,4,40,384]{3,2,0,1:T(8,128)(2,1)}, u32[]{:S(2)}, u32[]{:S(2)}) async-start(bf16[8,4,40,384]{3,2,0,1:T(8,128)(2,1)} %copy.52), calls=%async_computation.3 | async-start | bytes 1966080 | tf_op jit(solution)/shard_map/all_to_all | solution.py:80
  53.8 0.6 gather_fusion.4
  54.5 0.6 gather_fusion.3
  55.1 0.6 fusion.17
  59.6 0.6 fusion.16
  68.0 70.7 %all_gather.6 = bf16[1280,384]{1,0:T(8,128)(2,1)} all-gather(bf16[40,384]{1,0:T(8,128)(2,1)S(1)} %pad_maximum_fusion.1), channel_id=1, replica_groups=mesh['zh'=8,'zl'=4,'c'=2,'y'=4,'x'=4] {'zh','zl'}, dimensions={0}, use_global_device_ids=true | all-gather | bytes 1013760 | tf_op jit(solution)/shard_map/all_gather | solution.py:68
  138.7 21.3 %all-gather.2.cloned.1.call-done = bf16[2560,384]{1,0:T(8,128)(2,1)} async-done(((bf16[1280,384]{1,0:T(8,128)(2,1)}), bf16[2560,384]{1,0:T(8,128)(2,1)}) %all-gather.2.cloned.1.call-update) | async-done | bytes 1966096 | tf_op jit(solution)/shard_map/all_gather | solution.py:69
  160.0 1.7 copy.46
  161.7 2.3 convert_multiply_fusion
  164.4 1.6 pad_maximum_fusion
  166.0 6.8 %all-to-all-start.1 = ((bf16[16,260,160]{1,2,0:T(8,128)(2,1)}), bf16[16,260,160]{1,2,0:T(8,128)(2,1)S(1)}, u32[]{:S(2)}, u32[]{:S(2)}) async-start(bf16[16,260,160]{1,2,0:T(8,128)(2,1)} %pad_maximum_fusion), calls=%async_computation.1 | async-start | bytes 3932160 | tf_op jit(solution)/shard_map/all_to_all | solution.py:96
  172.8 2.1 reduce_sum.114
  174.9 29.4 %all-to-all-done.1 = bf16[16,260,160]{1,2,0:T(8,128)(2,1)S(1)} async-done(((bf16[16,260,160]{1,2,0:T(8,128)(2,1)}), bf16[16,260,160]{1,2,0:T(8,128)(2,1)S(1)}, u32[]{:S(2)}, u32[]{:S(2)}) %all-to-all-start.1) | async-done | bytes 1331232 | tf_op jit(solution)/shard_map/all_to_all | solution.py:96
  204.3 21.6 %all-to-all-start.4 = ((bf16[8,40,384]{2,1,0:T(8,128)(2,1)}), bf16[8,40,384]{2,1,0:T(8,128)(2,1)}, u32[]{:S(2)}, u32[]{:S(2)}) async-start(bf16[8,40,384]{2,1,0:T(8,128)(2,1)} %reduce_sum.114), calls=%async_computation.4 | async-start | bytes 491520 | tf_op jit(solution)/shard_map/all_to_all | solution.py:81
  225.9 3.1 %convolution_convert_fusion.1 = bf16[256,384]{1,0:T(8,128)(2,1)} fusion(bf16[2560,384]{1,0:T(8,128)(2,1)} %bitcast.50, f32[256]{0:T(256)S(1)} %add_rsqrt_fusion, bf16[256,2560]{0,1:T(8,128)(2,1)S(1)} %copy.40), kind=kOutput, calls=%fused_computation.17 | convolution fusion | flops 505380864 | bytes 3474432 | tf_op jit(solution)/shard_map/dot_general | solution.py:84
  229.1 0.4 copy.49
  229.8 1.6 multiply_convert_fusion
  231.4 32.6 %all-to-all-done.4 = bf16[8,40,384]{2,1,0:T(8,128)(2,1)} async-done(((bf16[8,40,384]{2,1,0:T(8,128)(2,1)}), bf16[8,40,384]{2,1,0:T(8,128)(2,1)}, u32[]{:S(2)}, u32[]{:S(2)}) %all-to-all-start.4) | async-done | bytes 245792 | tf_op jit(solution)/shard_map/all_to_all | solution.py:81
  264.0 1.6 convert_reduce_fusion.1
  (50 shorter events, 1.9 us)
Async XLA Ops:
  7.2 2.0 copy-start
  12.3 5.7 %copy-start.1 = (s32[48]{0:T(128)S(1)}, s32[48]{0:T(128)}, u32[]{:S(2)}) copy-start(s32[48]{0:T(128)} %param.8) | copy-start | bytes 580
  12.3 7.9 %copy-start.3 = (s32[6144]{0:T(1024)S(1)}, s32[6144]{0:T(1024)}, u32[]{:S(2)}) copy-start(s32[6144]{0:T(1024)} %param.7) | copy-start | bytes 73732
  12.3 8.5 %copy-start.4 = (bf16[40,512]{1,0:T(8,128)(2,1)S(1)}, bf16[40,512]{1,0:T(8,128)(2,1)}, u32[]{:S(2)}) copy-start(bf16[40,512]{1,0:T(8,128)(2,1)} %param.6) | copy-start | bytes 122884
  12.3 10.8 %all-to-all-start.2 = ((f32[8,4,2,40,384]{4,3,1,0,2:T(8,128)}), f32[8,4,2,40,384]{4,3,1,0,2:T(8,128)}, u32[]{:S(2)}, u32[]{:S(2)}) async-start(f32[8,4,2,40,384]{4,3,1,0,2:T(8,128)} %copy.51), calls=%async_computation.2 | async-start | bytes 7864320 | tf_op jit(solution)/shard_map/all_to_all | solution.py:79
  23.1 17.1 %all-to-all-start = ((bf16[16,40,256]{2,1,0:T(8,128)(2,1)}), bf16[16,40,256]{2,1,0:T(8,128)(2,1)S(1)}, u32[]{:S(2)}, u32[]{:S(2)}) async-start(bf16[16,40,256]{2,1,0:T(8,128)(2,1)} %fusion.4), calls=%async_computation | async-start | bytes 655360 | tf_op jit(solution)/shard_map/all_to_all | solution.py:56
  40.2 125.8 %all-to-all-start.3 = ((bf16[8,4,40,384]{3,2,0,1:T(8,128)(2,1)}), bf16[8,4,40,384]{3,2,0,1:T(8,128)(2,1)}, u32[]{:S(2)}, u32[]{:S(2)}) async-start(bf16[8,4,40,384]{3,2,0,1:T(8,128)(2,1)} %copy.52), calls=%async_computation.3 | async-start | bytes 1966080 | tf_op jit(solution)/shard_map/all_to_all | solution.py:80
  53.8 106.1 %all-gather.2.cloned.1.call-start = ((), (), s32[]{:S(2)}) async-start(), calls=%async_computation.5 | async-start | bytes 2949120 | tf_op jit(solution)/shard_map/all_gather | solution.py:69
  161.7 2.3 copy-start.2
  166.0 38.3 %all-to-all-start.1 = ((bf16[16,260,160]{1,2,0:T(8,128)(2,1)}), bf16[16,260,160]{1,2,0:T(8,128)(2,1)S(1)}, u32[]{:S(2)}, u32[]{:S(2)}) async-start(bf16[16,260,160]{1,2,0:T(8,128)(2,1)} %pad_maximum_fusion), calls=%async_computation.1 | async-start | bytes 3932160 | tf_op jit(solution)/shard_map/all_to_all | solution.py:96
  204.3 59.8 %all-to-all-start.4 = ((bf16[8,40,384]{2,1,0:T(8,128)(2,1)}), bf16[8,40,384]{2,1,0:T(8,128)(2,1)}, u32[]{:S(2)}, u32[]{:S(2)}) async-start(bf16[8,40,384]{2,1,0:T(8,128)(2,1)} %reduce_sum.114), calls=%async_computation.4 | async-start | bytes 491520 | tf_op jit(solution)/shard_map/all_to_all | solution.py:81
Sparse Core Ops, SparseCore 0:
  138.8 21.0 all-gather.1

commit v3 on v2

--- a/solution.py
+++ b/solution.py
@@ -19,7 +19,6 @@
 def _body(inputs, old_weight, keep_cols, owner, out_grad):
     n_t = lax.axis_size(TN)
     n_zh, n_zl, n_c = lax.axis_size("zh"), lax.axis_size("zl"), lax.axis_size("c")
-    n_z = n_zh * n_zl
     me = lax.axis_index(TN)
     blocks = owner.shape[0]
     own_blocks = blocks // n_t
@@ -53,21 +52,20 @@
     send = jnp.einsum(
         "rc,ctj->trj", old_weight, onehot, preferred_element_type=jnp.float32
     ).astype(old_weight.dtype)
-    recv = lax.all_to_all(send, TN, 0, 0, tiled=False)
+    send = jnp.broadcast_to(send[None], (n_c,) + send.shape).reshape(n_c * n_t, rows, 256)
+    recv = lax.all_to_all(send, ("c",) + TN, 0, 0, tiled=False)
 
     k_ids = jnp.arange(own_blocks, dtype=jnp.int32)
     mine_match = (owner[None, :] == me) & (owner_rank[None, :] == k_ids[:, None])
     my_blocks = jnp.sum(jnp.where(mine_match, block_ids[None, :], 0), axis=1)
     h_k = holder_of[my_blocks]
     s_k = slot_of[my_blocks]
-    recv4 = recv.reshape(n_t, rows, 2, 128)
-    new_stripe = jnp.concatenate(
-        [recv4[h_k[k], :, s_k[k], :] for k in range(own_blocks)], axis=1
-    )
+    recv5 = recv.reshape(n_c, n_t, rows, 2, 128)
+    chip_stripe = jnp.concatenate(
+        [recv5[:, h_k[k], :, s_k[k], :] for k in range(own_blocks)], axis=2
+    ).reshape(n_c * rows, -1)
 
-    piece = lax.all_gather(new_stripe, ("zh", "zl"), axis=0, tiled=True)
-    piece = lax.all_gather(piece, "c", axis=0, tiled=True)
-    piece = piece.reshape(n_c, n_z, rows, -1).transpose(1, 0, 2, 3).reshape(width, -1)
+    piece = lax.all_gather(chip_stripe, ("zh", "zl"), axis=0, tiled=True)
 
     x = inputs.astype(jnp.float32)
     inv = lax.rsqrt(jnp.mean(x * x, axis=1, keepdims=True) + 1e-05)
@@ -75,6 +73,7 @@
     normed = xhat.astype(jnp.bfloat16)
 
     wg = lax.dot_general(normed, out_grad, (((0,), (0,)), ((), ())), preferred_element_type=jnp.float32)
+    wg, _ = lax.optimization_barrier((wg, chip_stripe))
     wg = wg.reshape(n_zh, n_zl, n_c, rows, -1)
     wg = lax.all_to_all(wg, "c", 2, 2, tiled=False).sum(2)
     wg = lax.all_to_all(wg.astype(jnp.bfloat16), "zl", 1, 1, tiled=False).astype(jnp.float32).sum(1)

time: 273 us -> 293 us (1.073)
  waiting for transfers between devices: 89.7 us -> 181 us
  blocking collectives: 70.7 us -> 7.92 us
  starting transfers between devices: 54.8 us -> 40.6 us
  matrix products: 8.51 us -> 12 us
    all_gather x1, waiting for transfers between devices: 21.3 us -> 139 us  [_body(): piece = lax.all_gather(chip_stripe, ('zh', 'zl'), axis=0, tiled=True)]
    all_gather x1 -> x0, blocking collectives: 70.7 us -> none  [_body(): piece = lax.all_gather(new_stripe, ('zh', 'zl'), axis=0, tiled=True)]
    all_to_all x1, waiting for transfers between devices: 29.4 us -> 18 us  [_body(): got = lax.all_to_all(payload, TN, 0, 0, tiled=False)]
    all_to_all x1, waiting for transfers between devices: 32.6 us -> 23.1 us  [_body(): wg = lax.all_to_all(wg.astype(jnp.bfloat16), 'zh', 0, 0, tiled=False)]
    all_to_all x1, starting transfers between devices: 21.6 us -> 13.2 us  [_body(): wg = lax.all_to_all(wg.astype(jnp.bfloat16), 'zh', 0, 0, tiled=False)]
    all_to_all x0 -> x1, blocking collectives: none -> 7.92 us  [_body(): wg = lax.all_to_all(wg, 'c', 2, 2, tiled=False).sum(2)]
    all_to_all x2 -> x1, waiting for transfers between devices: 6.45 us -> 0.01 us  [_body(): recv = lax.all_to_all(send, ('c',) + TN, 0, 0, tiled=False)]
    all_to_all x2 -> x1, starting transfers between devices: 12.7 us -> 7.32 us  [_body(): recv = lax.all_to_all(send, ('c',) + TN, 0, 0, tiled=False)]
  transfers between devices with their start and end apart: 6 -> 5, of which waited for: 4 -> 3; matrix products, arithmetic and copies ran while one was open for 9% -> 7% of each run, Pallas kernels for 0% -> 0%
where the time goes in v3:
time: 293 us; the launch traced here: 292 us
  waiting for transfers between devices  181 us (62%)
  starting transfers between devices  40.6 us (14%)
  between operations  25.7 us (9%)
  other arithmetic  12.7 us (4%)
  local copies, waits for them, and re-layouts  12.3 us (4%)
  matrix products  12 us (4%)
  blocking collectives  7.92 us (3%)
    all_gather x1, waiting for transfers between devices, _body(): piece = lax.all_gather(chip_stripe, ('zh', 'zl'), axis=0, tiled=True)  139 us
    all_to_all x1, waiting for transfers between devices, _body(): wg = lax.all_to_all(wg.astype(jnp.bfloat16), 'zh', 0, 0, tiled=False)  23.1 us
    all_to_all x1, waiting for transfers between devices, _body(): got = lax.all_to_all(payload, TN, 0, 0, tiled=False)  18 us
    all_to_all x1, starting transfers between devices, _body(): lax.all_to_all(wg.astype(jnp.bfloat16), 'zl', 1, 1, tiled=False)  13.5 us
    all_to_all x1, starting transfers between devices, _body(): wg = lax.all_to_all(wg.astype(jnp.bfloat16), 'zh', 0, 0, tiled=False)  13.2 us
    all_to_all x1, blocking collectives, _body(): wg = lax.all_to_all(wg, 'c', 2, 2, tiled=False).sum(2)  7.92 us
    all_to_all x1, starting transfers between devices, _body(): recv = lax.all_to_all(send, ('c',) + TN, 0, 0, tiled=False)  7.32 us
    all_to_all x1, starting transfers between devices, _body(): got = lax.all_to_all(payload, TN, 0, 0, tiled=False)  6.61 us
  transfers between devices with their start and end apart: 5, of which 3 were waited for; matrix products, arithmetic and copies ran while one was open for 7% of the time, Pallas kernels for 0%

profile of v3, /device:TPU:32, one launch (start us, length us, event | category | flops | bytes accessed | tf_op | source)
XLA Modules:
  0.0 292.0 jit_solution(3341656254368159115)
XLA Ops:
  7.2 0.7 broadcast_compare_fusion
  7.9 0.9 convert_reduce_fusion.2
  9.0 1.3 gather_fusion
  10.3 0.6 gather_fusion.1
  11.5 1.3 gather_fusion.2
  12.8 2.3 fusion.4
  15.2 0.9 broadcast_in_dim.35
  16.1 7.3 %all-to-all-start = ((bf16[32,40,256]{2,1,0:T(8,128)(2,1)}), bf16[32,40,256]{2,1,0:T(8,128)(2,1)S(1)}, u32[]{:S(2)}, u32[]{:S(2)}) async-start(bf16[32,40,256]{2,1,0:T(8,128)(2,1)} %bitcast.6), calls=%async_computation | async-start | bytes 1310720 | tf_op jit(solution)/shard_map/all_to_all | solution.py:56
  23.4 0.6 gather_fusion.4
  24.0 0.6 gather_fusion.3
  24.7 0.6 fusion.17
  25.3 0.6 copy.31
  26.3 0.6 fusion.16
  38.4 2.7 fusion.6
  41.4 0.6 pad_maximum_fusion.1
  42.1 2.5 copy.38
  44.6 7.9 %all_to_all.25 = f32[8,4,2,40,384]{4,3,1,0,2:T(8,128)} all-to-all(f32[8,4,2,40,384]{4,3,1,0,2:T(8,128)S(1)} %copy.38), channel_id=1, replica_groups=mesh['zh'=8,'zl'=4,'c'=2,'y'=4,'x'=4] {'c'}, dimensions={2} | all-to-all | bytes 7864320 | tf_op jit(solution)/shard_map/all_to_all | solution.py:78
  52.5 2.5 reduce_sum.113
  55.0 1.1 copy.39
  56.1 13.5 %all-to-all-start.3 = ((bf16[8,4,40,384]{3,2,0,1:T(8,128)(2,1)}), bf16[8,4,40,384]{3,2,0,1:T(8,128)(2,1)}, u32[]{:S(2)}, u32[]{:S(2)}) async-start(bf16[8,4,40,384]{3,2,0,1:T(8,128)(2,1)} %copy.39), calls=%async_computation.3 | async-start | bytes 1966080 | tf_op jit(solution)/shard_map/all_to_all | solution.py:79
  69.6 0.7 all-gather.2.cloned.1.call-update
  70.3 138.9 %all-gather.2.cloned.1.call-done = bf16[2560,384]{1,0:T(8,128)(2,1)} async-done(((bf16[80,384]{1,0:T(8,128)(2,1)}), bf16[2560,384]{1,0:T(8,128)(2,1)}) %all-gather.2.cloned.1.call-update) | async-done | bytes 1966096 | tf_op jit(solution)/shard_map/all_gather | solution.py:68
  209.2 3.9 %convert_multiply_fusion = (f32[256,2560]{0,1:T(8,128)}, f32[256]{0:T(256)S(1)}, bf16[2560,256]{1,0:T(8,128)(2,1)S(1)}) fusion(bf16[256,2560]{0,1:T(8,128)(2,1)S(1)} %copy.31, f32[256]{0:T(256)S(1)} %add_rsqrt_fusion, bf16[2560,384]{1,0:T(8,128)(2,1)} %all-gather.2.cloned.1.call-done, bf16[256,384]{1,0:T(8,128)(2,1)S(1)} %copy-done), kind=kOutput, calls=%fused_computation.9 | convolution fusion | flops 507248384 | bytes 7407616 | tf_op jit(solution)/shard_map/dot_general | solution.py:85
  213.4 1.6 pad_maximum_fusion
  215.0 6.6 %all-to-all-start.1 = ((bf16[16,260,160]{1,2,0:T(8,128)(2,1)}), bf16[16,260,160]{1,2,0:T(8,128)(2,1)S(1)}, u32[]{:S(2)}, u32[]{:S(2)}) async-start(bf16[16,260,160]{1,2,0:T(8,128)(2,1)} %pad_maximum_fusion), calls=%async_computation.1 | async-start | bytes 3932160 | tf_op jit(solution)/shard_map/all_to_all | solution.py:95
  221.6 2.1 reduce_sum.114
  223.7 18.0 %all-to-all-done.1 = bf16[16,260,160]{1,2,0:T(8,128)(2,1)S(1)} async-done(((bf16[16,260,160]{1,2,0:T(8,128)(2,1)}), bf16[16,260,160]{1,2,0:T(8,128)(2,1)S(1)}, u32[]{:S(2)}, u32[]{:S(2)}) %all-to-all-start.1) | async-done | bytes 1331232 | tf_op jit(solution)/shard_map/all_to_all | solution.py:95
  241.7 13.2 %all-to-all-start.4 = ((bf16[8,40,384]{2,1,0:T(8,128)(2,1)}), bf16[8,40,384]{2,1,0:T(8,128)(2,1)}, u32[]{:S(2)}, u32[]{:S(2)}) async-start(bf16[8,40,384]{2,1,0:T(8,128)(2,1)} %reduce_sum.114), calls=%async_computation.4 | async-start | bytes 491520 | tf_op jit(solution)/shard_map/all_to_all | solution.py:80
  254.9 3.1 %convolution_convert_fusion.1 = bf16[256,384]{1,0:T(8,128)(2,1)} fusion(bf16[2560,384]{1,0:T(8,128)(2,1)} %all-gather.2.cloned.1.call-done, f32[256]{0:T(256)S(1)} %add_rsqrt_fusion, bf16[256,2560]{0,1:T(8,128)(2,1)S(1)} %copy.31), kind=kOutput, calls=%fused_computation.17 | convolution fusion | flops 505380864 | bytes 3474432 | tf_op jit(solution)/shard_map/dot_general | solution.py:83
  258.8 1.6 multiply_convert_fusion
  260.4 23.1 %all-to-all-done.4 = bf16[8,40,384]{2,1,0:T(8,128)(2,1)} async-done(((bf16[8,40,384]{2,1,0:T(8,128)(2,1)}), bf16[8,40,384]{2,1,0:T(8,128)(2,1)}, u32[]{:S(2)}, u32[]{:S(2)}) %all-to-all-start.4) | async-done | bytes 245792 | tf_op jit(solution)/shard_map/all_to_all | solution.py:80
  283.6 1.6 convert_reduce_fusion.1
  (42 shorter events, 2.6 us)
Async XLA Ops:
  7.2 31.2 %copy-start = (bf16[256,384]{1,0:T(8,128)(2,1)S(1)}, bf16[256,384]{1,0:T(8,128)(2,1)}, u32[]{:S(2)}) copy-start(bf16[256,384]{1,0:T(8,128)(2,1)} %param.9) | copy-start | bytes 589828
  15.2 10.1 %copy-start.1 = (bf16[256,2560]{1,0:T(8,128)(2,1)S(1)}, bf16[256,2560]{1,0:T(8,128)(2,1)}, u32[]{:S(2)}) copy-start(bf16[256,2560]{1,0:T(8,128)(2,1)} %param.5) | copy-start | bytes 3932164
  16.1 25.0 %all-to-all-start = ((bf16[32,40,256]{2,1,0:T(8,128)(2,1)}), bf16[32,40,256]{2,1,0:T(8,128)(2,1)S(1)}, u32[]{:S(2)}, u32[]{:S(2)}) async-start(bf16[32,40,256]{2,1,0:T(8,128)(2,1)} %bitcast.6), calls=%async_computation | async-start | bytes 1310720 | tf_op jit(solution)/shard_map/all_to_all | solution.py:56
  56.1 158.9 %all-to-all-start.3 = ((bf16[8,4,40,384]{3,2,0,1:T(8,128)(2,1)}), bf16[8,4,40,384]{3,2,0,1:T(8,128)(2,1)}, u32[]{:S(2)}, u32[]{:S(2)}) async-start(bf16[8,4,40,384]{3,2,0,1:T(8,128)(2,1)} %copy.39), calls=%async_computation.3 | async-start | bytes 1966080 | tf_op jit(solution)/shard_map/all_to_all | solution.py:79
  69.6 139.6 %all-gather.2.cloned.1.call-start = ((), (), s32[]{:S(2)}) async-start(), calls=%async_computation.5 | async-start | bytes 2027520 | tf_op jit(solution)/shard_map/all_gather | solution.py:68
  215.0 26.7 %all-to-all-start.1 = ((bf16[16,260,160]{1,2,0:T(8,128)(2,1)}), bf16[16,260,160]{1,2,0:T(8,128)(2,1)S(1)}, u32[]{:S(2)}, u32[]{:S(2)}) async-start(bf16[16,260,160]{1,2,0:T(8,128)(2,1)} %pad_maximum_fusion), calls=%async_computation.1 | async-start | bytes 3932160 | tf_op jit(solution)/shard_map/all_to_all | solution.py:95
  241.7 41.8 %all-to-all-start.4 = ((bf16[8,40,384]{2,1,0:T(8,128)(2,1)}), bf16[8,40,384]{2,1,0:T(8,128)(2,1)}, u32[]{:S(2)}, u32[]{:S(2)}) async-start(bf16[8,40,384]{2,1,0:T(8,128)(2,1)} %reduce_sum.114), calls=%async_computation.4 | async-start | bytes 491520 | tf_op jit(solution)/shard_map/all_to_all | solution.py:80
Sparse Core Ops, SparseCore 0:
  73.6 135.5 all-gather.1

commit v4 on v2

--- a/solution.py
+++ b/solution.py
@@ -66,7 +66,8 @@
     )
 
     piece = lax.all_gather(new_stripe, ("zh", "zl"), axis=0, tiled=True)
-    piece = lax.all_gather(piece, "c", axis=0, tiled=True)
+    piece = jnp.broadcast_to(piece[None], (n_c,) + piece.shape)
+    piece = lax.all_to_all(piece, "c", 0, 0, tiled=False)
     piece = piece.reshape(n_c, n_z, rows, -1).transpose(1, 0, 2, 3).reshape(width, -1)
 
     x = inputs.astype(jnp.float32)
@@ -76,7 +77,7 @@
 
     wg = lax.dot_general(normed, out_grad, (((0,), (0,)), ((), ())), preferred_element_type=jnp.float32)
     wg = wg.reshape(n_zh, n_zl, n_c, rows, -1)
-    wg = lax.all_to_all(wg, "c", 2, 2, tiled=False).sum(2)
+    wg = lax.all_to_all(wg.astype(jnp.bfloat16), "c", 2, 2, tiled=False).astype(jnp.float32).sum(2)
     wg = lax.all_to_all(wg.astype(jnp.bfloat16), "zl", 1, 1, tiled=False).astype(jnp.float32).sum(1)
     wg = lax.all_to_all(wg.astype(jnp.bfloat16), "zh", 0, 0, tiled=False)
     wg = wg.astype(jnp.float32).sum(0)

time: 273 us -> 235 us (0.86)
  the two profiles are of different devices: /device:TPU:32 before, /device:TPU:24 now
where the time goes in v4:
time: 235 us; the launch traced here: 234 us
  waiting for transfers between devices  76.1 us (32%)
  blocking collectives  69.1 us (29%)
  starting transfers between devices  44.6 us (19%)
  between operations  12.5 us (5%)
  local copies, waits for them, and re-layouts  12.4 us (5%)
  other arithmetic  9.77 us (4%)
  matrix products  9.39 us (4%)
    all_gather x1, blocking collectives, _body(): piece = lax.all_gather(new_stripe, ('zh', 'zl'), axis=0, tiled=True)  63.8 us
    all_to_all x1, waiting for transfers between devices, _body(): wg = lax.all_to_all(wg.astype(jnp.bfloat16), 'zh', 0, 0, tiled=False)  30.6 us
    all_to_all x1, waiting for transfers between devices, _body(): got = lax.all_to_all(payload, TN, 0, 0, tiled=False)  25 us
    all_to_all x1, waiting for transfers between devices, _body(): lax.all_to_all(wg.astype(jnp.bfloat16), 'zl', 1, 1, tiled=False)  20.5 us
    all_to_all x1, starting transfers between devices, _body(): recv = lax.all_to_all(send, TN, 0, 0, tiled=False)  16.8 us
    all_to_all x1, starting transfers between devices, _body(): wg = lax.all_to_all(wg.astype(jnp.bfloat16), 'zh', 0, 0, tiled=False)  12.4 us
    all_to_all x1, starting transfers between devices, _body(): got = lax.all_to_all(payload, TN, 0, 0, tiled=False)  7.23 us
    all_to_all x1, blocking collectives, _body(): piece = lax.all_to_all(piece, 'c', 0, 0, tiled=False)  5.31 us
  transfers between devices with their start and end apart: 5, of which 3 were waited for; matrix products, arithmetic and copies ran while one was open for 10% of the time, Pallas kernels for 0%

profile of v4, /device:TPU:24, one launch (start us, length us, event | category | flops | bytes accessed | tf_op | source)
XLA Modules:
  0.0 233.9 jit_solution(5152247173859023209)
XLA Ops:
  0.6 1.6 copy.46
  2.3 0.4 fusion.2
  2.7 0.9 convolution_convert_fusion
  3.5 1.5 copy.57
  5.0 3.9 %all-to-all-start.3 = ((bf16[8,4,2,40,384]{4,3,1,0,2:T(8,128)(2,1)}), bf16[8,4,2,40,384]{4,3,1,0,2:T(8,128)(2,1)S(1)}, u32[]{:S(2)}, u32[]{:S(2)}) async-start(bf16[8,4,2,40,384]{4,3,1,0,2:T(8,128)(2,1)} %copy.57), calls=%async_computation.3 | async-start | bytes 3932160 | tf_op jit(solution)/shard_map/all_to_all | solution.py:80
  9.3 0.6 gather_fusion
  9.9 0.6 gather_fusion.1
  11.1 0.6 gather_fusion.2
  11.8 3.1 %fusion.4 = bf16[16,40,256]{2,1,0:T(8,128)(2,1)} fusion(s32[16,256]{1,0:T(8,128)S(1)} %min.12, bf16[40,512]{1,0:T(8,128)(2,1)} %param.6), kind=kOutput, calls=%fused_computation.17 | convolution fusion | flops 170033152 | bytes 385024 | tf_op jit(solution)/shard_map/rc,ctj->trj/dot_general | solution.py:53
  14.8 16.8 %all-to-all-start = ((bf16[16,40,256]{2,1,0:T(8,128)(2,1)}), bf16[16,40,256]{2,1,0:T(8,128)(2,1)}, u32[]{:S(2)}, u32[]{:S(2)}) async-start(bf16[16,40,256]{2,1,0:T(8,128)(2,1)} %fusion.4), calls=%async_computation | async-start | bytes 655360 | tf_op jit(solution)/shard_map/all_to_all | solution.py:56
  31.7 0.6 gather_fusion.4
  32.3 0.6 gather_fusion.3
  33.0 0.6 fusion.16
  37.4 0.7 fusion.15
  42.0 1.6 reduce_sum.116
  43.5 2.3 copy.58
  49.7 1.1 reshape.185
  50.9 63.8 %all_gather.3 = bf16[1280,384]{1,0:T(8,128)(2,1)S(1)} all-gather(bf16[40,384]{1,0:T(8,128)(2,1)S(1)} %pad_maximum_fusion.1), channel_id=1, replica_groups=mesh['zh'=8,'zl'=4,'c'=2,'y'=4,'x'=4] {'zh','zl'}, dimensions={0}, use_global_device_ids=true | all-gather | bytes 1013760 | tf_op jit(solution)/shard_map/all_gather | solution.py:68
  114.8 5.3 %all_to_all.30 = bf16[2,1280,384]{2,1,0:T(8,128)(2,1)S(1)} all-to-all(bf16[2,1280,384]{2,1,0:T(8,128)(2,1)S(1)} %broadcast_in_dim.41), channel_id=1, replica_groups=mesh['zh'=8,'zl'=4,'c'=2,'y'=4,'x'=4] {'c'}, dimensions={0} | all-to-all | bytes 3932160 | tf_op jit(solution)/shard_map/all_to_all | solution.py:70
  120.1 4.2 %all-to-all-start.4 = ((bf16[8,4,40,384]{3,2,0,1:T(8,128)(2,1)}), bf16[8,4,40,384]{3,2,0,1:T(8,128)(2,1)}, u32[]{:S(2)}, u32[]{:S(2)}) async-start(bf16[8,4,40,384]{3,2,0,1:T(8,128)(2,1)} %copy.58), calls=%async_computation.4 | async-start | bytes 1966080 | tf_op jit(solution)/shard_map/all_to_all | solution.py:81
  124.6 2.4 %convert_multiply_fusion = (f32[256,2560]{0,1:T(8,128)}, f32[256]{0:T(256)S(1)}, bf16[2560,256]{1,0:T(8,128)(2,1)S(1)}) fusion(bf16[256,2560]{0,1:T(8,128)(2,1)S(1)} %copy.46, f32[256]{0:T(256)S(1)} %add_rsqrt_fusion, bf16[2560,384]{1,0:T(8,128)(2,1)S(1)} %bitcast.50, bf16[256,384]{1,0:T(8,128)(2,1)S(1)} %copy-done), kind=kOutput, calls=%fused_computation.10 | convolution fusion | flops 507248384 | bytes 7407616 | tf_op jit(solution)/shard_map/dot_general | solution.py:87
  127.3 1.6 pad_maximum_fusion
  128.9 20.5 %all-to-all-done.4 = bf16[8,4,40,384]{3,2,0,1:T(8,128)(2,1)} async-done(((bf16[8,4,40,384]{3,2,0,1:T(8,128)(2,1)}), bf16[8,4,40,384]{3,2,0,1:T(8,128)(2,1)}, u32[]{:S(2)}, u32[]{:S(2)}) %all-to-all-start.4) | async-done | bytes 983072 | tf_op jit(solution)/shard_map/all_to_all | solution.py:81
  149.3 7.2 %all-to-all-start.2 = ((bf16[16,260,160]{1,2,0:T(8,128)(2,1)}), bf16[16,260,160]{1,2,0:T(8,128)(2,1)S(1)}, u32[]{:S(2)}, u32[]{:S(2)}) async-start(bf16[16,260,160]{1,2,0:T(8,128)(2,1)} %pad_maximum_fusion), calls=%async_computation.2 | async-start | bytes 3932160 | tf_op jit(solution)/shard_map/all_to_all | solution.py:97
  156.6 2.1 reduce_sum.117
  158.7 25.0 %all-to-all-done.2 = bf16[16,260,160]{1,2,0:T(8,128)(2,1)S(1)} async-done(((bf16[16,260,160]{1,2,0:T(8,128)(2,1)}), bf16[16,260,160]{1,2,0:T(8,128)(2,1)S(1)}, u32[]{:S(2)}, u32[]{:S(2)}) %all-to-all-start.2) | async-done | bytes 1331232 | tf_op jit(solution)/shard_map/all_to_all | solution.py:97
  183.7 12.4 %all-to-all-start.5 = ((bf16[8,40,384]{2,1,0:T(8,128)(2,1)}), bf16[8,40,384]{2,1,0:T(8,128)(2,1)}, u32[]{:S(2)}, u32[]{:S(2)}) async-start(bf16[8,40,384]{2,1,0:T(8,128)(2,1)} %reduce_sum.117), calls=%async_computation.5 | async-start | bytes 491520 | tf_op jit(solution)/shard_map/all_to_all | solution.py:82
  196.1 3.1 %convolution_convert_fusion.2 = bf16[256,384]{1,0:T(8,128)(2,1)} fusion(bf16[2560,384]{1,0:T(8,128)(2,1)} %bitcast.51, f32[256]{0:T(256)S(1)} %add_rsqrt_fusion, bf16[256,2560]{0,1:T(8,128)(2,1)S(1)} %copy.46), kind=kOutput, calls=%fused_computation.18 | convolution fusion | flops 505380864 | bytes 3474432 | tf_op jit(solution)/shard_map/dot_general | solution.py:85
  199.3 0.4 copy.55
  200.1 1.6 multiply_convert_fusion
  201.6 30.6 %all-to-all-done.5 = bf16[8,40,384]{2,1,0:T(8,128)(2,1)} async-done(((bf16[8,40,384]{2,1,0:T(8,128)(2,1)}), bf16[8,40,384]{2,1,0:T(8,128)(2,1)}, u32[]{:S(2)}, u32[]{:S(2)}) %all-to-all-start.5) | async-done | bytes 245792 | tf_op jit(solution)/shard_map/all_to_all | solution.py:82
  232.2 1.6 convert_reduce_fusion.1
  (47 shorter events, 2.2 us)
Async XLA Ops:
  0.6 2.0 copy-start
  5.0 3.9 %copy-start.1 = (s32[48]{0:T(128)S(1)}, s32[48]{0:T(128)}, u32[]{:S(2)}) copy-start(s32[48]{0:T(128)} %param.8) | copy-start | bytes 580
  5.0 6.1 %copy-start.3 = (s32[6144]{0:T(1024)S(1)}, s32[6144]{0:T(1024)}, u32[]{:S(2)}) copy-start(s32[6144]{0:T(1024)} %param.7) | copy-start | bytes 73732
  5.0 9.8 %all-to-all-start.3 = ((bf16[8,4,2,40,384]{4,3,1,0,2:T(8,128)(2,1)}), bf16[8,4,2,40,384]{4,3,1,0,2:T(8,128)(2,1)S(1)}, u32[]{:S(2)}, u32[]{:S(2)}) async-start(bf16[8,4,2,40,384]{4,3,1,0,2:T(8,128)(2,1)} %copy.57), calls=%async_computation.3 | async-start | bytes 3932160 | tf_op jit(solution)/shard_map/all_to_all | solution.py:80
  14.8 34.9 %all-to-all-start = ((bf16[16,40,256]{2,1,0:T(8,128)(2,1)}), bf16[16,40,256]{2,1,0:T(8,128)(2,1)}, u32[]{:S(2)}, u32[]{:S(2)}) async-start(bf16[16,40,256]{2,1,0:T(8,128)(2,1)} %fusion.4), calls=%async_computation | async-start | bytes 655360 | tf_op jit(solution)/shard_map/all_to_all | solution.py:56
  120.1 29.2 %all-to-all-start.4 = ((bf16[8,4,40,384]{3,2,0,1:T(8,128)(2,1)}), bf16[8,4,40,384]{3,2,0,1:T(8,128)(2,1)}, u32[]{:S(2)}, u32[]{:S(2)}) async-start(bf16[8,4,40,384]{3,2,0,1:T(8,128)(2,1)} %copy.58), calls=%async_computation.4 | async-start | bytes 1966080 | tf_op jit(solution)/shard_map/all_to_all | solution.py:81
  124.6 2.4 %copy-start.2 = (bf16[32,2,40,384]{3,2,1,0:T(8,128)(2,1)}, bf16[32,2,40,384]{3,2,1,0:T(8,128)(2,1)S(1)}, u32[]{:S(2)}) copy-start(bf16[32,2,40,384]{3,2,1,0:T(8,128)(2,1)S(1)} %copy.52) | copy-start | bytes 5898244
  149.3 34.4 %all-to-all-start.2 = ((bf16[16,260,160]{1,2,0:T(8,128)(2,1)}), bf16[16,260,160]{1,2,0:T(8,128)(2,1)S(1)}, u32[]{:S(2)}, u32[]{:S(2)}) async-start(bf16[16,260,160]{1,2,0:T(8,128)(2,1)} %pad_maximum_fusion), calls=%async_computation.2 | async-start | bytes 3932160 | tf_op jit(solution)/shard_map/all_to_all | solution.py:97
  183.7 48.5 %all-to-all-start.5 = ((bf16[8,40,384]{2,1,0:T(8,128)(2,1)}), bf16[8,40,384]{2,1,0:T(8,128)(2,1)}, u32[]{:S(2)}, u32[]{:S(2)}) async-start(bf16[8,40,384]{2,1,0:T(8,128)(2,1)} %reduce_sum.117), calls=%async_computation.5 | async-start | bytes 491520 | tf_op jit(solution)/shard_map/all_to_all | solution.py:82

commit v5 on v4

--- a/solution.py
+++ b/solution.py
@@ -76,9 +76,8 @@
     normed = xhat.astype(jnp.bfloat16)
 
     wg = lax.dot_general(normed, out_grad, (((0,), (0,)), ((), ())), preferred_element_type=jnp.float32)
-    wg = wg.reshape(n_zh, n_zl, n_c, rows, -1)
-    wg = lax.all_to_all(wg.astype(jnp.bfloat16), "c", 2, 2, tiled=False).astype(jnp.float32).sum(2)
-    wg = lax.all_to_all(wg.astype(jnp.bfloat16), "zl", 1, 1, tiled=False).astype(jnp.float32).sum(1)
+    wg = wg.reshape(n_zh, n_zl * n_c, rows, -1)
+    wg = lax.all_to_all(wg.astype(jnp.bfloat16), ("zl", "c"), 1, 1, tiled=False).astype(jnp.float32).sum(1)
     wg = lax.all_to_all(wg.astype(jnp.bfloat16), "zh", 0, 0, tiled=False)
     wg = wg.astype(jnp.float32).sum(0)
 

time: 235 us -> 250 us (1.064)
  the two profiles are of different devices: /device:TPU:24 before, /device:TPU:32 now
where the time goes in v5:
time: 250 us; the launch traced here: 249 us
  waiting for transfers between devices  94.4 us (38%)
  blocking collectives  77.8 us (31%)
  starting transfers between devices  32.7 us (13%)
  between operations  12.4 us (5%)
  local copies, waits for them, and re-layouts  12.1 us (5%)
  other arithmetic  10.3 us (4%)
  matrix products  9.88 us (4%)
    all_gather x1, blocking collectives, _body(): piece = lax.all_gather(new_stripe, ('zh', 'zl'), axis=0, tiled=True)  71.6 us
    all_to_all x1, waiting for transfers between devices, _body(): lax.all_to_all(wg.astype(jnp.bfloat16), ('zl', 'c'), 1, 1, tiled=False)  35 us
    all_to_all x1, waiting for transfers between devices, _body(): wg = lax.all_to_all(wg.astype(jnp.bfloat16), 'zh', 0, 0, tiled=False)  29.8 us
    all_to_all x1, waiting for transfers between devices, _body(): got = lax.all_to_all(payload, TN, 0, 0, tiled=False)  29.6 us
    all_to_all x1, starting transfers between devices, _body(): wg = lax.all_to_all(wg.astype(jnp.bfloat16), 'zh', 0, 0, tiled=False)  12.9 us
    all_to_all x1, starting transfers between devices, _body(): got = lax.all_to_all(payload, TN, 0, 0, tiled=False)  7.24 us
    all_to_all x1, starting transfers between devices, _body(): recv = lax.all_to_all(send, TN, 0, 0, tiled=False)  7.03 us
    all_to_all x1, blocking collectives, _body(): piece = lax.all_to_all(piece, 'c', 0, 0, tiled=False)  6.18 us
  transfers between devices with their start and end apart: 4, of which 3 were waited for; matrix products, arithmetic and copies ran while one was open for 9% of the time, Pallas kernels for 0%

profile of v5, /device:TPU:32, one launch (start us, length us, event | category | flops | bytes accessed | tf_op | source)
XLA Modules:
  0.0 249.5 jit_solution(8937768430449794557)
XLA Ops:
  0.7 0.7 broadcast_compare_fusion
  1.4 0.9 convert_reduce_fusion.2
  2.5 1.3 gather_fusion
  3.8 0.6 gather_fusion.1
  5.0 1.3 gather_fusion.2
  6.3 3.1 %fusion.4 = bf16[16,40,256]{2,1,0:T(8,128)(2,1)} fusion(s32[16,256]{1,0:T(8,128)S(1)} %min.12, bf16[40,512]{1,0:T(8,128)(2,1)} %param.6), kind=kOutput, calls=%fused_computation.17 | convolution fusion | flops 170033152 | bytes 385024 | tf_op jit(solution)/shard_map/rc,ctj->trj/dot_general | solution.py:53
  9.4 7.0 %all-to-all-start = ((bf16[16,40,256]{2,1,0:T(8,128)(2,1)}), bf16[16,40,256]{2,1,0:T(8,128)(2,1)S(1)}, u32[]{:S(2)}, u32[]{:S(2)}) async-start(bf16[16,40,256]{2,1,0:T(8,128)(2,1)} %fusion.4), calls=%async_computation | async-start | bytes 655360 | tf_op jit(solution)/shard_map/all_to_all | solution.py:56
  16.5 0.6 gather_fusion.4
  17.1 0.6 gather_fusion.3
  17.8 0.6 fusion.16
  22.3 0.6 fusion.15
  26.6 0.6 copy.34
  27.6 0.8 convolution_convert_fusion
  28.5 1.5 copy.45
  34.1 71.6 %all_gather.3 = bf16[1280,384]{1,0:T(8,128)(2,1)S(1)} all-gather(bf16[40,384]{1,0:T(8,128)(2,1)S(1)} %pad_maximum_fusion.1), channel_id=1, replica_groups=mesh['zh'=8,'zl'=4,'c'=2,'y'=4,'x'=4] {'zh','zl'}, dimensions={0}, use_global_device_ids=true | all-gather | bytes 1013760 | tf_op jit(solution)/shard_map/all_gather | solution.py:68
  105.9 6.2 %all_to_all.25 = bf16[2,1280,384]{2,1,0:T(8,128)(2,1)} all-to-all(bf16[2,1280,384]{2,1,0:T(8,128)(2,1)S(1)} %broadcast_in_dim.41), channel_id=1, replica_groups=mesh['zh'=8,'zl'=4,'c'=2,'y'=4,'x'=4] {'c'}, dimensions={0} | all-to-all | bytes 3932160 | tf_op jit(solution)/shard_map/all_to_all | solution.py:70
  112.0 5.6 %all-to-all-start.3 = ((bf16[8,8,40,384]{3,2,0,1:T(8,128)(2,1)}), bf16[8,8,40,384]{3,2,0,1:T(8,128)(2,1)S(1)}, u32[]{:S(2)}, u32[]{:S(2)}) async-start(bf16[8,8,40,384]{3,2,0,1:T(8,128)(2,1)} %copy.45), calls=%async_computation.3 | async-start | bytes 3932160 | tf_op jit(solution)/shard_map/all_to_all | solution.py:80
  117.6 1.7 copy.40
  119.4 2.8 %convert_multiply_fusion = (f32[256,2560]{0,1:T(8,128)}, f32[256]{0:T(256)S(1)}, bf16[2560,256]{1,0:T(8,128)(2,1)}) fusion(bf16[256,2560]{0,1:T(8,128)(2,1)S(1)} %copy.34, f32[256]{0:T(256)S(1)} %add_rsqrt_fusion, bf16[2560,384]{1,0:T(8,128)(2,1)S(1)} %bitcast.50, bf16[256,384]{1,0:T(8,128)(2,1)S(1)} %copy-done), kind=kOutput, calls=%fused_computation.10 | convolution fusion | flops 507248384 | bytes 7407616 | tf_op jit(solution)/shard_map/dot_general | solution.py:86
  122.6 2.9 %pad_maximum_fusion = bf16[16,260,160]{1,2,0:T(8,128)(2,1)} fusion(bf16[16,4,160]{1,2,0:T(8,128)(2,1)S(1)} %broadcast_in_dim.44, bf16[16,256,160]{1,2,0:T(8,128)(2,1)} %bitcast.52), kind=kLoop, calls=%fused_computation.15 | loop fusion | flops 2662400 | bytes 2662400 | tf_op jit(solution)/shard_map/concatenate | solution.py:95
  125.4 35.0 %all-to-all-done.3 = bf16[8,8,40,384]{3,2,0,1:T(8,128)(2,1)S(1)} async-done(((bf16[8,8,40,384]{3,2,0,1:T(8,128)(2,1)}), bf16[8,8,40,384]{3,2,0,1:T(8,128)(2,1)S(1)}, u32[]{:S(2)}, u32[]{:S(2)}) %all-to-all-start.3) | async-done | bytes 1966112 | tf_op jit(solution)/shard_map/all_to_all | solution.py:80
  160.4 7.2 %all-to-all-start.2 = ((bf16[16,260,160]{1,2,0:T(8,128)(2,1)}), bf16[16,260,160]{1,2,0:T(8,128)(2,1)}, u32[]{:S(2)}, u32[]{:S(2)}) async-start(bf16[16,260,160]{1,2,0:T(8,128)(2,1)} %pad_maximum_fusion), calls=%async_computation.2 | async-start | bytes 3932160 | tf_op jit(solution)/shard_map/all_to_all | solution.py:96
  167.7 1.0 reduce_sum.104
  168.7 29.6 %all-to-all-done.2 = bf16[16,260,160]{1,2,0:T(8,128)(2,1)} async-done(((bf16[16,260,160]{1,2,0:T(8,128)(2,1)}), bf16[16,260,160]{1,2,0:T(8,128)(2,1)}, u32[]{:S(2)}, u32[]{:S(2)}) %all-to-all-start.2) | async-done | bytes 1331232 | tf_op jit(solution)/shard_map/all_to_all | solution.py:96
  198.3 12.9 %all-to-all-start.4 = ((bf16[8,40,384]{2,1,0:T(8,128)(2,1)}), bf16[8,40,384]{2,1,0:T(8,128)(2,1)S(1)}, u32[]{:S(2)}, u32[]{:S(2)}) async-start(bf16[8,40,384]{2,1,0:T(8,128)(2,1)} %reduce_sum.104), calls=%async_computation.4 | async-start | bytes 491520 | tf_op jit(solution)/shard_map/all_to_all | solution.py:81
  211.1 3.1 %convolution_convert_fusion.2 = bf16[256,384]{1,0:T(8,128)(2,1)} fusion(bf16[2560,384]{1,0:T(8,128)(2,1)} %bitcast.51, f32[256]{0:T(256)S(1)} %add_rsqrt_fusion, bf16[256,2560]{0,1:T(8,128)(2,1)S(1)} %copy.34), kind=kOutput, calls=%fused_computation.18 | convolution fusion | flops 505380864 | bytes 3474432 | tf_op jit(solution)/shard_map/dot_general | solution.py:84
  214.2 1.1 slice.55
  215.4 0.4 copy.43
  215.9 1.5 convert_reduce_fusion
  217.4 1.6 multiply_convert_fusion
  219.0 29.8 %all-to-all-done.4 = bf16[8,40,384]{2,1,0:T(8,128)(2,1)S(1)} async-done(((bf16[8,40,384]{2,1,0:T(8,128)(2,1)}), bf16[8,40,384]{2,1,0:T(8,128)(2,1)S(1)}, u32[]{:S(2)}, u32[]{:S(2)}) %all-to-all-start.4) | async-done | bytes 245792 | tf_op jit(solution)/shard_map/all_to_all | solution.py:81
  248.8 0.7 convert_reduce_fusion.1
  (41 shorter events, 1.9 us)
Async XLA Ops:
  0.6 27.0 %copy-start = (bf16[256,384]{1,0:T(8,128)(2,1)S(1)}, bf16[256,384]{1,0:T(8,128)(2,1)}, u32[]{:S(2)}) copy-start(bf16[256,384]{1,0:T(8,128)(2,1)} %param.9) | copy-start | bytes 589828
  6.3 20.3 %copy-start.2 = (bf16[256,2560]{1,0:T(8,128)(2,1)S(1)}, bf16[256,2560]{1,0:T(8,128)(2,1)}, u32[]{:S(2)}) copy-start(bf16[256,2560]{1,0:T(8,128)(2,1)} %param.5) | copy-start | bytes 3932164
  9.4 24.4 %all-to-all-start = ((bf16[16,40,256]{2,1,0:T(8,128)(2,1)}), bf16[16,40,256]{2,1,0:T(8,128)(2,1)S(1)}, u32[]{:S(2)}, u32[]{:S(2)}) async-start(bf16[16,40,256]{2,1,0:T(8,128)(2,1)} %fusion.4), calls=%async_computation | async-start | bytes 655360 | tf_op jit(solution)/shard_map/all_to_all | solution.py:56
  112.0 48.4 %all-to-all-start.3 = ((bf16[8,8,40,384]{3,2,0,1:T(8,128)(2,1)}), bf16[8,8,40,384]{3,2,0,1:T(8,128)(2,1)S(1)}, u32[]{:S(2)}, u32[]{:S(2)}) async-start(bf16[8,8,40,384]{3,2,0,1:T(8,128)(2,1)} %copy.45), calls=%async_computation.3 | async-start | bytes 3932160 | tf_op jit(solution)/shard_map/all_to_all | solution.py:80
  119.4 2.8 %copy-start.1 = (bf16[32,2,40,384]{3,2,1,0:T(8,128)(2,1)}, bf16[32,2,40,384]{3,2,1,0:T(8,128)(2,1)S(1)}, u32[]{:S(2)}) copy-start(bf16[32,2,40,384]{3,2,1,0:T(8,128)(2,1)S(1)} %copy.40) | copy-start | bytes 5898244
  160.4 37.9 %all-to-all-start.2 = ((bf16[16,260,160]{1,2,0:T(8,128)(2,1)}), bf16[16,260,160]{1,2,0:T(8,128)(2,1)}, u32[]{:S(2)}, u32[]{:S(2)}) async-start(bf16[16,260,160]{1,2,0:T(8,128)(2,1)} %pad_maximum_fusion), calls=%async_computation.2 | async-start | bytes 3932160 | tf_op jit(solution)/shard_map/all_to_all | solution.py:96
  198.3 50.6 %all-to-all-start.4 = ((bf16[8,40,384]{2,1,0:T(8,128)(2,1)}), bf16[8,40,384]{2,1,0:T(8,128)(2,1)S(1)}, u32[]{:S(2)}, u32[]{:S(2)}) async-start(bf16[8,40,384]{2,1,0:T(8,128)(2,1)} %reduce_sum.104), calls=%async_computation.4 | async-start | bytes 491520 | tf_op jit(solution)/shard_map/all_to_all | solution.py:81
